TPU v7x, 32 devices: a whole 2x2x4 slice. The times are simulated.
32 devices in a mesh: tm: 8 (over z, y), cal: 4 (over x, core).
Axes of the slice: x: 2, y: 2, z: 4, core: 2. Of those that a mesh axis runs over, the one named last changes fastest.
Arguments:
- src_design: float32 [5, 4096, 128], P(None, ('tm', 'cal')), may hold values from -6 to 6
- att_design: float32 [3, 4096, 128], P(None, ('tm', 'cal')), may hold values from -6 to 6
- obs_phase: float32 [4096, 128], P(('tm', 'cal')), may hold values from 0 to 1
- cal_design: float32 [4096, 128], P(('tm', 'cal')), may hold values from -6 to 6
- obs_weight: float32 [4096, 128], P(('tm', 'cal')), may hold values from 0.1 to 12
- knot_index: int32 [4096, 128], P(('tm', 'cal')), may hold values from 0 to 4092, as said below
- cal_block: int32 [4096, 128], P(('tm', 'cal')), may hold values from 0 to 7
- cal_column: int32 [4096, 128], P(('tm', 'cal')), may hold values from 0 to 4095
- obs_count: int32 [4096], P(('tm', 'cal')), may hold values from 32 to 128
- src_res: float32 [5, 4096], P(None, ('tm', 'cal')), may hold values from -6 to 6
- att_res: float32 [3, 4096], P(None, ('tm', 'cal')), may hold values from -6 to 6
- cal_res: float32 [8, 4096], P('cal'), may hold values from -6 to 6
- src_dir: float32 [5, 4096], P(None, ('tm', 'cal')), may hold values from -6 to 6
- att_dir: float32 [3, 4096], P(None, ('tm', 'cal')), may hold values from -6 to 6
- cal_dir: float32 [8, 4096], P('cal'), may hold values from -6 to 6
Outputs:
- new_src_res: float32 [5, 4096], P(None, ('tm', 'cal'))
- new_att_res: float32 [3, 4096], P(None, ('tm', 'cal'))
- new_cal_res: float32 [8, 4096], P('cal')
- new_src_dir: float32 [5, 4096], P(None, ('tm', 'cal'))
- new_att_dir: float32 [3, 4096], P(None, ('tm', 'cal'))
- new_cal_dir: float32 [8, 4096], P('cal')
Inputs may be any that keep to these rules, and one draw needn't show every extreme that they name: The observations of source row s have knot intervals from (s // 128) * 128 to (s // 128) * 128 + 127, and knot_index + 3 < 4096.
All inputs are finite; a program needn't handle non-finite values.
Results may differ from a plain program's by a relative error of at most 0.00015.
Values sent between devices are 32-bit elements; how exact they have to be, the bound alone decides.
No kernel may reach another device: no remote copies, remote signals or barrier semaphores. Data moves between devices by JAX's collectives and lax.ppermute only.
A program may use at most 64 MiB of HBM per device.

v0:
```python
import jax
import jax.numpy as jnp
from jax import lax
from jax.sharding import PartitionSpec as P

EXACT = lax.Precision.HIGHEST


def passed_along(block, axis, distance):
    devices = range(lax.axis_size(axis))
    route = [(i - distance, i) for i in devices if i - distance in devices]
    return lax.ppermute(block, axis, route)


def spline(phase):
    rest = 1.0 - phase
    cube = phase * phase * phase
    square = phase * phase
    first = rest * rest * rest / 6.0
    second = (3.0 * cube - 6.0 * square + 4.0) / 6.0
    third = (-3.0 * cube + 3.0 * square + 3.0 * phase + 1.0) / 6.0
    fourth = cube / 6.0
    return (first, second, third, fourth)


def local(
    src_design,
    att_design,
    obs_phase,
    cal_design,
    obs_weight,
    knot_index,
    cal_block,
    cal_column,
    obs_count,
    src_res,
    att_res,
    cal_res,
    src_dir,
    att_dir,
    cal_dir,
):
    knot_count = att_dir.shape[1]
    blocks, col_width = cal_dir.shape
    all_blocks = blocks * lax.axis_size("cal")
    cal_size = all_blocks * col_width
    lane = 128
    rows = cal_size // lane
    src_rows, slots = obs_phase.shape
    first_row = (lax.axis_index("tm") == 0).astype(jnp.float32)
    cal_values = lax.all_gather(cal_dir, "cal", axis=0, tiled=True)
    edge_knots = passed_along(att_dir[:, :3], ("tm", "cal"), -1)
    att_ext = jnp.concatenate([att_dir, edge_knots], axis=1)
    live_mask = (lax.broadcasted_iota(jnp.int32, obs_phase.shape, 1) < obs_count[:, None]).astype(
        jnp.float32
    )
    basis = spline(obs_phase)
    local_knot = knot_index - lax.axis_index(("tm", "cal")) * knot_count
    knot_iota = lax.broadcasted_iota(jnp.int32, (knot_count, 1, 1), 0)
    knot_hot = (local_knot[None] == knot_iota).astype(jnp.float32)
    table = jnp.stack([att_ext[:, m : m + knot_count].T for m in range(4)], axis=1)
    table = table.reshape(knot_count, 12)
    picked = jnp.einsum("jq,jso->qso", table, knot_hot, precision=EXACT).reshape(
        4, 3, src_rows, slots
    )
    y_att = jnp.zeros_like(obs_phase)
    for m in range(4):
        y_att = y_att + basis[m] * jnp.sum(att_design * picked[m], axis=0)
    flat_index = cal_block * col_width + cal_column
    high = flat_index // lane
    low = flat_index % lane
    high_hot = (high[None] == lax.broadcasted_iota(jnp.int32, (rows, 1, 1), 0)).astype(jnp.float32)
    low_hot = (low[None] == lax.broadcasted_iota(jnp.int32, (lane, 1, 1), 0)).astype(jnp.float32)
    cal_table = cal_values.reshape(rows, lane)
    row_vals = jnp.einsum("hl,hso->lso", cal_table, high_hot, precision=EXACT)
    y_cal = cal_design * jnp.sum(row_vals * low_hot, axis=0)
    y_src = jnp.sum(src_design * src_dir[:, :, None], axis=0)
    response = live_mask * (y_src + y_att + y_cal)
    weighted = obs_weight * response
    curv_local = jnp.sum(weighted * response)
    norm_local = (
        jnp.sum(src_res * src_res)
        + jnp.sum(att_res * att_res)
        + first_row * jnp.sum(cal_res * cal_res)
    )
    q_src = jnp.sum(src_design * weighted[None], axis=2)
    scaled = att_design * weighted[None]
    spread = jnp.stack([basis[m][None] * scaled for m in range(4)], axis=0).reshape(
        12, src_rows, slots
    )
    gathered = jnp.einsum("qso,jso->jq", spread, knot_hot, precision=EXACT).reshape(
        knot_count, 4, 3
    )
    grad_ext = jnp.zeros((3, knot_count + 3), jnp.float32)
    for m in range(4):
        grad_ext = grad_ext + jnp.pad(gathered[:, m, :].T, ((0, 0), (m, 3 - m)))
    incoming = passed_along(grad_ext[:, knot_count:], ("tm", "cal"), 1)
    q_att = jnp.concatenate([grad_ext[:, :3] + incoming, grad_ext[:, 3:knot_count]], axis=1)
    cal_weighted = (cal_design * weighted)[None] * low_hot
    cal_term = jnp.einsum("hso,lso->hl", high_hot, cal_weighted, precision=EXACT)
    scalars = jnp.zeros((1, lane), jnp.float32).at[0, 0].set(norm_local).at[0, 1].set(curv_local)
    packed = jnp.concatenate([cal_term, scalars], axis=0)
    summed = lax.psum(packed, ("tm", "cal"))
    norm_now = summed[rows, 0]
    curvature = summed[rows, 1]
    own = lax.axis_index("cal") * (blocks * col_width // lane)
    q_cal = lax.dynamic_slice_in_dim(summed, own, blocks * col_width // lane, 0).reshape(
        blocks, col_width
    )
    step_len = norm_now / curvature
    new_src_res = src_res - step_len * q_src
    new_att_res = att_res - step_len * q_att
    new_cal_res = cal_res - step_len * q_cal
    next_local = (
        jnp.sum(new_src_res * new_src_res)
        + jnp.sum(new_att_res * new_att_res)
        + first_row * jnp.sum(new_cal_res * new_cal_res)
    )
    norm_next = lax.psum(jnp.zeros((1, lane), jnp.float32).at[0, 0].set(next_local), ("tm", "cal"))[
        0, 0
    ]
    ratio = norm_next / norm_now
    return (
        new_src_res,
        new_att_res,
        new_cal_res,
        new_src_res + ratio * src_dir,
        new_att_res + ratio * att_dir,
        new_cal_res + ratio * cal_dir,
    )


def solution(mesh):
    return jax.shard_map(
        local,
        mesh=mesh,
        in_specs=(
            P(None, ("tm", "cal"), None),
            P(None, ("tm", "cal"), None),
            P(("tm", "cal"), None),
            P(("tm", "cal"), None),
            P(("tm", "cal"), None),
            P(("tm", "cal"), None),
            P(("tm", "cal"), None),
            P(("tm", "cal"), None),
            P(("tm", "cal")),
            P(None, ("tm", "cal")),
            P(None, ("tm", "cal")),
            P("cal", None),
            P(None, ("tm", "cal")),
            P(None, ("tm", "cal")),
            P("cal", None),
        ),
        out_specs=(
            P(None, ("tm", "cal")),
            P(None, ("tm", "cal")),
            P("cal", None),
            P(None, ("tm", "cal")),
            P(None, ("tm", "cal")),
            P("cal", None),
        ),
        check_vma=False,
    )
```

profile of v0, /device:TPU:0, one launch (start us, length us, event | category | flops | bytes accessed | tf_op | source)
XLA Modules:
  0.0 323.5 jit_solution(16515309153429786869)
XLA Ops:
  7.2 0.0 all-reduce.8.cloned.1.call-start
  7.2 1.3 collective-permute-start
  8.5 0.6 compare_reduce_fusion.1
  9.2 0.6 compare_reduce_fusion
  9.8 0.7 constant_dynamic-update-slice_fusion.1
  10.5 1.4 multiply_reduce_fusion.4
  11.9 1.3 multiply_reduce_fusion.8
  13.2 1.3 multiply_reduce_fusion.6
  17.1 0.6 slice.117
  17.7 0.8 broadcast_subtract_fusion
  18.5 0.1 copy.49
  18.6 7.7 %all-gather = f32[4,2,4096]{2,1,0:T(2,128)S(1)} all-gather(f32[1,2,4096]{2,1,0:T(2,128)} %bitcast.78), channel_id=1, replica_groups=mesh['tm'=8,'cal'=4] {'cal'}, dimensions={0}, use_global_device_ids=true | all-gather | bytes 163840 | tf_op jit(solution)/shard_map/all_gather | solution.py:51
  26.2 0.1 reshape.140
  26.4 0.9 add_select_fusion.1
  27.3 0.1 copy.48
  27.4 1.3 iota_compare_fusion.1
  28.7 38.5 %copy.50 = pred[128,128,128]{2,0,1:T(32,128)(4,1)S(1)} copy(pred[128,128,128]{1,0,2:T(32,128)(4,1)S(1)} %iota_compare_fusion.1) | data formatting | bytes 4194304 | tf_op jit(solution)/shard_map/eq | solution.py:60
  67.2 2.7 iota_compare_fusion
  69.9 0.0 copy-start
  69.9 0.0 copy-start.9
  70.0 20.5 %copy.55 = pred[256,128,128]{2,0,1:T(32,128)(4,1)} copy(pred[256,128,128]{1,0,2:T(32,128)(4,1)S(1)} %iota_compare_fusion) | data formatting | bytes 8388608 | tf_op jit(solution)/shard_map/eq | solution.py:72
  90.5 0.0 copy-done
  90.5 0.1 multiply_reduce_fusion.1
  90.7 0.0 copy-start.8
  90.7 0.0 copy-start.1
  90.7 8.2 %fusion = f32[128,128]{1,0:T(8,128)S(1)} fusion(s32[128,128]{1,0:T(8,128)S(1)} %get-tuple-element.62, pred[256,128,128]{2,0,1:T(32,128)(4,1)} %copy.55, f32[256,128]{1,0:T(8,128)S(1)} %reshape.140), kind=kOutput, calls=%fused_computation.2 | convolution fusion | flops 6448726016 | bytes 4456448 | tf_op jit(solution)/shard_map/hl,hso->lso/dot_general | solution.py:75
  98.9 0.0 copy-start.5
  98.9 0.0 copy-start.6
  98.9 0.0 copy-start.7
  99.0 0.0 copy-start.14
  99.0 0.0 collective-permute-done
  99.0 0.1 slice_bitcast_fusion.2
  99.1 2.2 fusion.29
  101.3 0.8 fusion.7
  102.1 0.0 copy-done.5
  102.1 0.0 copy-done.6
  102.2 0.1 fusion.25
  102.3 0.2 multiply_reduce_fusion
  102.4 0.1 multiply_bitcast_fusion.3
  102.5 0.1 maximum_bitcast_fusion
  102.6 0.3 copy.59
  102.9 4.2 %fusion.4 = f32[128,4,3]{0,1,2:T(4,128)S(1)} fusion(f32[4,3,128,128]{3,0,2,1:T(4,128)S(1)} %copy.59, s32[128,128]{0,1:T(8,128)S(1)} %copy.49), kind=kOutput, calls=%fused_computation.9 | convolution fusion | flops 304087040 | bytes 858112 | tf_op jit(solution)/shard_map/qso,jso->jq/dot_general | solution.py:91
  107.1 0.1 pad_add_fusion
  107.2 0.1 slice.143
  107.3 0.6 multiply_reduce_fusion.2
  107.9 2.2 collective-permute-start.1
  110.1 4.7 %fusion.1 = f32[128,128,128]{2,0,1:T(8,128)} fusion(f32[128,128]{1,0:T(8,128)S(1)} %get-tuple-element.52, s32[128,128]{1,0:T(8,128)S(1)} %get-tuple-element.62), kind=kLoop, calls=%fused_computation.5 | loop fusion | flops 4194304 | bytes 8519680 | tf_op jit(solution)/shard_map/mul | solution.py:99
  114.8 9.3 %copy.57 = f32[128,128,128]{1,0,2:T(8,128)} copy(f32[128,128,128]{2,0,1:T(8,128)} %fusion.1) | data formatting | bytes 16777216 | tf_op jit(solution)/shard_map/mul | solution.py:99
  124.2 11.2 %convolution_bitcast_fusion = f32[256,128]{1,0:T(8,128)S(1)} fusion(f32[128,128,128]{1,0,2:T(8,128)} %copy.57, s32[128,128]{0,1:T(8,128)S(1)} %copy.48), kind=kOutput, calls=%fused_computation.8 | convolution fusion | flops 6446645248 | bytes 8585216 | tf_op jit(solution)/shard_map/hso,lso->hl/dot_general | solution.py:100
  135.3 2.5 fusion.28
  137.9 1.4 scatter.11
  139.3 0.7 pad_maximum_fusion
  139.9 0.0 all-reduce.8.cloned.1.call-update
  140.0 0.0 collective-permute-done.1
  140.0 123.3 %all-reduce.8.cloned.1.call-done = f32[257,128]{1,0:T(8,128)} async-done(((f32[257,128]{1,0:T(8,128)}), f32[257,128]{1,0:T(8,128)}) %all-reduce.8.cloned.1.call-update) | async-done | bytes 131600 | tf_op jit(solution)/shard_map/psum | solution.py:103
  263.3 1.3 fusion.26
  266.0 0.8 dynamic-slice_multiply_fusion
  266.8 0.6 multiply_reduce_fusion.5
  267.4 0.7 multiply_reduce_fusion.3
  268.8 0.8 multiply_reduce_fusion.7
  271.6 42.5 %psum.15 = f32[1,128]{1,0:T(1,128)S(1)} all-reduce(f32[1,128]{1,0:T(1,128)S(1)} %scatter.14), channel_id=1, replica_groups=mesh['tm'=8,'cal'=4] {'tm','cal'}, use_global_device_ids=true, to_apply=%region_17.18 | all-reduce | flops 128 | bytes 1024 | tf_op jit(solution)/shard_map/psum | solution.py:119
  314.8 0.6 multiply_add_fusion.3
  315.4 0.6 multiply_add_fusion.2
  316.0 0.6 multiply_add_fusion.1
  (31 shorter events, 0.1 us)
Async XLA Ops:
  7.2 256.2 %all-reduce.8.cloned.1.call-start = ((), (), s32[]{:S(2)}) async-start(), calls=%async_computation | async-start | bytes 270336 | tf_op jit(solution)/shard_map/psum | solution.py:103
  7.2 91.8 %collective-permute-start = (f32[3,3]{1,0:T(4,128)}, f32[3,3]{1,0:T(4,128)S(1)}, u32[]{:S(2)}, u32[]{:S(2)}) collective-permute-start(f32[3,3]{1,0:T(4,128)} %bitcast.79), channel_id=1, source_target_pairs={{1,0},{2,1},{3,2},{4,3},{5,4},{6,5},{7,6},{8,7},{9,8},{10,9},{11,1... | collective-permute-start | bytes 116 | tf_op jit(solution)/shard_map/ppermute | solution.py:12
  69.9 20.6 %copy-start = (f32[5,128,128]{2,1,0:T(8,128)S(1)}, f32[5,128,128]{2,1,0:T(8,128)}, u32[]{:S(2)}) copy-start(f32[5,128,128]{2,1,0:T(8,128)} %param.21) | copy-start | bytes 983044
  69.9 20.6 %copy-start.9 = (f32[5,128]{1,0:T(8,128)S(1)}, f32[5,128]{1,0:T(8,128)}, u32[]{:S(2)}) copy-start(f32[5,128]{1,0:T(8,128)} %param.33) | copy-start | bytes 7684
  90.7 8.4 %copy-start.8 = (f32[3,128]{1,0:T(4,128)S(1)}, f32[3,128]{1,0:T(4,128)}, u32[]{:S(2)}) copy-start(f32[3,128]{1,0:T(4,128)} %param.34) | copy-start | bytes 4612
  90.7 10.6 %copy-start.1 = (f32[3,128,128]{2,1,0:T(8,128)S(1)}, f32[3,128,128]{2,1,0:T(8,128)}, u32[]{:S(2)}) copy-start(f32[3,128,128]{2,1,0:T(8,128)} %param.22) | copy-start | bytes 589828
  98.9 3.2 copy-start.5
  98.9 3.2 copy-start.6
  98.9 3.2 copy-start.7
  99.0 3.2 copy-start.14
  107.9 32.1 %collective-permute-start.1 = (f32[3,3]{1,0:T(4,128)S(1)}, f32[3,3]{1,0:T(4,128)S(1)}, u32[]{:S(2)}, u32[]{:S(2)}) collective-permute-start(f32[3,3]{1,0:T(4,128)S(1)} %slice.142), channel_id=1, source_target_pairs={{0,1},{1,2},{2,3},{3,4},{4,5},{5,6},{6,7},{7,8},{8,9},{9,10},{10,1... | collective-permute-start | bytes 116 | tf_op jit(solution)/shard_map/ppermute | solution.py:12
  124.2 142.6 %copy-start.11 = (f32[5,128]{1,0:T(8,128)S(1)}, f32[5,128]{1,0:T(8,128)}, u32[]{:S(2)}) copy-start(f32[5,128]{1,0:T(8,128)} %param.30) | copy-start | bytes 7684
  124.2 143.3 %copy-start.4 = (f32[2,4096]{1,0:T(2,128)S(1)}, f32[2,4096]{1,0:T(2,128)}, u32[]{:S(2)}) copy-start(f32[2,4096]{1,0:T(2,128)} %param.32) | copy-start | bytes 98308
  124.2 144.7 %copy-start.12 = (f32[3,128]{1,0:T(4,128)S(1)}, f32[3,128]{1,0:T(4,128)}, u32[]{:S(2)}) copy-start(f32[3,128]{1,0:T(4,128)} %param.31) | copy-start | bytes 4612
  124.2 191.8 %copy-start.2 = (f32[2,4096]{1,0:T(2,128)S(1)}, f32[2,4096]{1,0:T(2,128)}, u32[]{:S(2)}) copy-start(f32[2,4096]{1,0:T(2,128)} %param.35) | copy-start | bytes 98308
  267.4 49.2 %copy-start.10 = (f32[5,128]{1,0:T(8,128)}, f32[5,128]{1,0:T(8,128)S(1)}, u32[]{:S(2)}) copy-start(f32[5,128]{1,0:T(8,128)S(1)} %get-tuple-element.51) | copy-start | bytes 7684
  268.1 48.5 %copy-start.3 = (f32[2,4096]{1,0:T(2,128)}, f32[2,4096]{1,0:T(2,128)S(1)}, u32[]{:S(2)}) copy-start(f32[2,4096]{1,0:T(2,128)S(1)} %get-tuple-element.47) | copy-start | bytes 98308
  269.6 47.1 %copy-start.13 = (f32[3,128]{1,0:T(4,128)}, f32[3,128]{1,0:T(4,128)S(1)}, u32[]{:S(2)}) copy-start(f32[3,128]{1,0:T(4,128)S(1)} %get-tuple-element.49) | copy-start | bytes 4612
Sparse Core Ops, SparseCore 0:
  140.1 123.1 all-reduce.7
where the time goes:
time: 324 us
  waiting for transfers between devices  123 us (38%)
  local copies, waits for them, and re-layouts  73.3 us (23%)
  blocking collectives  50.1 us (15%)
  matrix products  25.8 us (8%)
  other arithmetic  25.7 us (8%)
  between operations  21.7 us (7%)
  starting transfers between devices  3.56 us (1%)
    psum x1, waiting for transfers between devices, local(): summed = lax.psum(packed, ('tm', 'cal'))  123 us
    psum x1, blocking collectives, local(): lax.psum(jnp.zeros((1, lane), jnp.float32).at[0, 0].set(next_local), ('tm...  42.5 us
    eq x1, local copies, waits for them, and re-layouts, local(): knot_hot = (local_knot[None] == knot_iota).astype(jnp.float32)  38.5 us
    eq x1, local copies, waits for them, and re-layouts, local(): high[None] == lax.broadcasted_iota(jnp.int32, (rows, 1, 1), 0)  20.5 us
    dot_general x1, matrix products, local(): jnp.einsum('hso,lso->hl', high_hot, cal_weighted, precision=EXACT)  11.2 us
    mul x1, local copies, waits for them, and re-layouts, local(): cal_weighted = (cal_design * weighted)[None] * low_hot  9.32 us
    dot_general x1, matrix products, local(): row_vals = jnp.einsum('hl,hso->lso', cal_table, high_hot, precision=EXACT)  8.23 us
    all_gather x1, blocking collectives, local(): cal_values = lax.all_gather(cal_dir, 'cal', axis=0, tiled=True)  7.65 us
  transfers between devices with their start and end apart: 3, of which 1 were waited for; matrix products, arithmetic and copies ran while one was open for 34% of the time, Pallas kernels for 0%

commit v1 on v0

--- a/solution.py
+++ b/solution.py
@@ -48,7 +48,14 @@
     rows = cal_size // lane
     src_rows, slots = obs_phase.shape
     first_row = (lax.axis_index("tm") == 0).astype(jnp.float32)
-    cal_values = lax.all_gather(cal_dir, "cal", axis=0, tiled=True)
+    size = lax.axis_size("cal")
+    right = [(i_2, (i_2 + 1) % size) for i_2 in range(size)]
+    parts = [cal_dir]
+    for stride in range(1, size):
+        parts = [lax.ppermute(parts[0], "cal", right), *parts]
+    out = jnp.concatenate(parts, axis=0)
+    shift = (lax.axis_index("cal") + 1) * parts[-1].shape[0]
+    cal_values = jnp.roll(out, shift, axis=0)
     edge_knots = passed_along(att_dir[:, :3], ("tm", "cal"), -1)
     att_ext = jnp.concatenate([att_dir, edge_knots], axis=1)
     live_mask = (lax.broadcasted_iota(jnp.int32, obs_phase.shape, 1) < obs_count[:, None]).astype(

time: 324 us -> 323 us (level)
  blocking collectives: 50.1 us -> 42.5 us
  starting transfers between devices: 3.56 us -> 7.34 us
    all_gather x1 -> x0, blocking collectives: 7.65 us -> none  [local(): cal_values = lax.all_gather(cal_dir, 'cal', axis=0, tiled=True)]
    ppermute x0 -> x3, starting transfers between devices: none -> 4.51 us  [local(): parts = [lax.ppermute(parts[0], 'cal', right), *parts]]
  transfers between devices with their start and end apart: 3 -> 6, of which waited for: 1 -> 2; matrix products, arithmetic and copies ran while one was open for 34% -> 32% of each run, Pallas kernels for 0% -> 0%
where the time goes in v1:
time: 323 us; the launch traced here: 322 us
  waiting for transfers between devices  126 us (39%)
  local copies, waits for them, and re-layouts  73.5 us (23%)
  blocking collectives  42.5 us (13%)
  other arithmetic  25.7 us (8%)
  matrix products  25.5 us (8%)
  between operations  21.7 us (7%)
  starting transfers between devices  7.34 us (2%)
    psum x1, waiting for transfers between devices, local(): summed = lax.psum(packed, ('tm', 'cal'))  124 us
    psum x1, blocking collectives, local(): lax.psum(jnp.zeros((1, lane), jnp.float32).at[0, 0].set(next_local), ('tm...  42.5 us
    eq x1, local copies, waits for them, and re-layouts, local(): knot_hot = (local_knot[None] == knot_iota).astype(jnp.float32)  38.6 us
    eq x1, local copies, waits for them, and re-layouts, local(): high[None] == lax.broadcasted_iota(jnp.int32, (rows, 1, 1), 0)  20.5 us
    dot_general x1, matrix products, local(): jnp.einsum('hso,lso->hl', high_hot, cal_weighted, precision=EXACT)  11.1 us
    mul x1, local copies, waits for them, and re-layouts, local(): cal_weighted = (cal_design * weighted)[None] * low_hot  9.32 us
    dot_general x1, matrix products, local(): row_vals = jnp.einsum('hl,hso->lso', cal_table, high_hot, precision=EXACT)  8.26 us
  transfers between devices with their start and end apart: 6, of which 2 were waited for; matrix products, arithmetic and copies ran while one was open for 32% of the time, Pallas kernels for 0%

profile of v1, /device:TPU:0, one launch (start us, length us, event | category | flops | bytes accessed | tf_op | source)
XLA Modules:
  0.0 322.1 jit_solution(10112204643191235756)
XLA Ops:
  7.2 0.0 all-reduce.8.cloned.1.call-start
  7.2 1.3 collective-permute-start
  8.5 1.2 collective-permute-start.1
  9.7 0.6 compare_reduce_fusion.1
  10.3 0.6 compare_reduce_fusion
  11.0 0.7 constant_dynamic-update-slice_fusion.1
  11.7 1.4 multiply_reduce_fusion.4
  13.0 1.3 multiply_reduce_fusion.8
  14.3 1.3 multiply_reduce_fusion.6
  18.2 0.6 slice.117
  18.8 0.8 broadcast_subtract_fusion
  19.7 0.1 copy.34
  19.8 0.9 add_select_fusion.1
  20.7 0.1 copy.33
  20.8 1.3 iota_compare_fusion.1
  22.2 38.6 %copy.35 = pred[128,128,128]{2,0,1:T(32,128)(4,1)S(1)} copy(pred[128,128,128]{1,0,2:T(32,128)(4,1)S(1)} %iota_compare_fusion.1) | data formatting | bytes 4194304 | tf_op jit(solution)/shard_map/eq | solution.py:67
  60.7 2.7 iota_compare_fusion
  63.4 0.0 copy-start
  63.4 0.0 copy-start.9
  63.4 0.0 copy-start.8
  63.4 0.0 copy-start.1
  63.5 20.5 %copy.41 = pred[256,128,128]{2,0,1:T(32,128)(4,1)} copy(pred[256,128,128]{1,0,2:T(32,128)(4,1)S(1)} %iota_compare_fusion) | data formatting | bytes 8388608 | tf_op jit(solution)/shard_map/eq | solution.py:79
  84.0 0.1 multiply_reduce_fusion.1
  84.2 0.1 slice_bitcast_fusion.2
  84.3 0.0 collective-permute-done.1
  84.3 2.8 collective-permute-start.2
  87.1 2.1 fusion.28
  89.2 0.0 collective-permute-done.2
  89.2 0.5 collective-permute-start.3
  89.8 0.8 fusion.6
  90.6 2.0 collective-permute-done.3
  92.6 0.2 concatenate.22
  92.9 0.0 copy-start.5
  92.9 0.0 copy-start.6
  92.9 0.0 copy-start.7
  92.9 0.0 copy-start.14
  93.0 8.3 %select_reduce_fusion = f32[128,128]{1,0:T(8,128)S(1)} fusion(s32[128,128]{1,0:T(8,128)S(1)} %get-tuple-element.62, pred[256,128,128]{2,0,1:T(32,128)(4,1)} %copy.41, f32[256,128]{1,0:T(8,128)S(1)} %reshape.140), kind=kOutput, calls=%fused_computation.1 | convolution fusion | flops 6448726016 | bytes 4456448 | tf_op jit(solution)/shard_map/hl,hso->lso/dot_general | solution.py:82
  101.3 0.1 fusion.24
  101.4 0.2 multiply_reduce_fusion
  101.5 0.1 multiply_bitcast_fusion.3
  101.6 0.1 maximum_bitcast_fusion
  101.7 0.3 copy.44
  102.0 4.0 %fusion.3 = f32[128,4,3]{0,1,2:T(4,128)S(1)} fusion(f32[4,3,128,128]{3,0,2,1:T(4,128)S(1)} %copy.44, s32[128,128]{0,1:T(8,128)S(1)} %copy.34), kind=kOutput, calls=%fused_computation.8 | convolution fusion | flops 304087040 | bytes 858112 | tf_op jit(solution)/shard_map/qso,jso->jq/dot_general | solution.py:98
  106.0 0.1 pad_add_fusion
  106.1 0.1 slice.143
  106.2 0.6 multiply_reduce_fusion.2
  106.8 1.5 collective-permute-start.4
  108.3 4.7 %fusion = f32[128,128,128]{2,0,1:T(8,128)} fusion(f32[128,128]{1,0:T(8,128)S(1)} %get-tuple-element.52, s32[128,128]{1,0:T(8,128)S(1)} %get-tuple-element.62), kind=kLoop, calls=%fused_computation.4 | loop fusion | flops 4194304 | bytes 8519680 | tf_op jit(solution)/shard_map/mul | solution.py:106
  113.0 9.3 %copy.42 = f32[128,128,128]{1,0,2:T(8,128)} copy(f32[128,128,128]{2,0,1:T(8,128)} %fusion) | data formatting | bytes 16777216 | tf_op jit(solution)/shard_map/mul | solution.py:106
  122.3 11.1 %convolution_bitcast_fusion = f32[256,128]{1,0:T(8,128)S(1)} fusion(f32[128,128,128]{1,0,2:T(8,128)} %copy.42, s32[128,128]{0,1:T(8,128)S(1)} %copy.33), kind=kOutput, calls=%fused_computation.7 | convolution fusion | flops 6446645248 | bytes 8585216 | tf_op jit(solution)/shard_map/hso,lso->hl/dot_general | solution.py:107
  133.5 2.5 fusion.27
  136.0 1.4 scatter.11
  137.4 0.7 pad_maximum_fusion
  138.1 0.0 all-reduce.8.cloned.1.call-update
  138.1 123.8 %all-reduce.8.cloned.1.call-done = f32[257,128]{1,0:T(8,128)} async-done(((f32[257,128]{1,0:T(8,128)}), f32[257,128]{1,0:T(8,128)}) %all-reduce.8.cloned.1.call-update) | async-done | bytes 131600 | tf_op jit(solution)/shard_map/psum | solution.py:110
  261.9 1.3 fusion.25
  264.6 0.8 dynamic-slice_multiply_fusion
  265.4 0.6 multiply_reduce_fusion.5
  266.0 0.7 multiply_reduce_fusion.3
  267.4 0.8 multiply_reduce_fusion.7
  270.2 42.5 %psum.15 = f32[1,128]{1,0:T(1,128)S(1)} all-reduce(f32[1,128]{1,0:T(1,128)S(1)} %scatter.14), channel_id=1, replica_groups=mesh['tm'=8,'cal'=4] {'tm','cal'}, use_global_device_ids=true, to_apply=%region_17.18 | all-reduce | flops 128 | bytes 1024 | tf_op jit(solution)/shard_map/psum | solution.py:126
  313.4 0.6 multiply_add_fusion.3
  314.0 0.6 multiply_add_fusion.2
  314.6 0.6 multiply_add_fusion.1
  (38 shorter events, 0.2 us)
Async XLA Ops:
  7.2 254.7 %all-reduce.8.cloned.1.call-start = ((), (), s32[]{:S(2)}) async-start(), calls=%async_computation | async-start | bytes 270336 | tf_op jit(solution)/shard_map/psum | solution.py:110
  7.2 77.0 %collective-permute-start = (f32[3,3]{1,0:T(4,128)}, f32[3,3]{1,0:T(4,128)S(1)}, u32[]{:S(2)}, u32[]{:S(2)}) collective-permute-start(f32[3,3]{1,0:T(4,128)} %bitcast.73), channel_id=1, source_target_pairs={{1,0},{2,1},{3,2},{4,3},{5,4},{6,5},{7,6},{8,7},{9,8},{10,9},{11,1... | collective-permute-start | bytes 116 | tf_op jit(solution)/shard_map/ppermute | solution.py:12
  8.5 75.8 %collective-permute-start.1 = (f32[2,4096]{1,0:T(2,128)}, f32[2,4096]{1,0:T(2,128)S(1)}, u32[]{:S(2)}, u32[]{:S(2)}) collective-permute-start(f32[2,4096]{1,0:T(2,128)} %param.35), channel_id=1, source_target_pairs={{0,1},{1,2},{2,3},{3,0},{4,5},{5,6},{6,7},{7,4},{8,9},{9,10},{10,1... | collective-permute-start | bytes 98312 | tf_op jit(solution)/shard_map/ppermute | solution.py:55
  63.4 20.6 %copy-start = (f32[5,128,128]{2,1,0:T(8,128)S(1)}, f32[5,128,128]{2,1,0:T(8,128)}, u32[]{:S(2)}) copy-start(f32[5,128,128]{2,1,0:T(8,128)} %param.21) | copy-start | bytes 983044
  63.4 20.6 %copy-start.9 = (f32[5,128]{1,0:T(8,128)S(1)}, f32[5,128]{1,0:T(8,128)}, u32[]{:S(2)}) copy-start(f32[5,128]{1,0:T(8,128)} %param.33) | copy-start | bytes 7684
  63.4 20.8 %copy-start.8 = (f32[3,128]{1,0:T(4,128)S(1)}, f32[3,128]{1,0:T(4,128)}, u32[]{:S(2)}) copy-start(f32[3,128]{1,0:T(4,128)} %param.34) | copy-start | bytes 4612
  63.4 26.3 %copy-start.1 = (f32[3,128,128]{2,1,0:T(8,128)S(1)}, f32[3,128,128]{2,1,0:T(8,128)}, u32[]{:S(2)}) copy-start(f32[3,128,128]{2,1,0:T(8,128)} %param.22) | copy-start | bytes 589828
  84.0 8.6 %copy-start.2 = (f32[2,4096]{1,0:T(2,128)S(1)}, f32[2,4096]{1,0:T(2,128)}, u32[]{:S(2)}) copy-start(f32[2,4096]{1,0:T(2,128)} %param.35) | copy-start | bytes 98308
  84.3 4.9 %collective-permute-start.2 = (f32[2,4096]{1,0:T(2,128)S(1)}, f32[2,4096]{1,0:T(2,128)S(1)}, u32[]{:S(2)}, u32[]{:S(2)}) collective-permute-start(f32[2,4096]{1,0:T(2,128)S(1)} %collective-permute-done.1), channel_id=1, source_target_pairs={{0,1},{1,2},{2,3},{3,0},{4,5},{5,6},{6,7},{7,4},{8,9},{9,10},{10,1... | collective-permute-start | bytes 98312 | tf_op jit(solution)/shard_map/ppermute | solution.py:55
  89.2 3.4 %collective-permute-start.3 = (f32[2,4096]{1,0:T(2,128)S(1)}, f32[2,4096]{1,0:T(2,128)S(1)}, u32[]{:S(2)}, u32[]{:S(2)}) collective-permute-start(f32[2,4096]{1,0:T(2,128)S(1)} %collective-permute-done.2), channel_id=1, source_target_pairs={{0,1},{1,2},{2,3},{3,0},{4,5},{5,6},{6,7},{7,4},{8,9},{9,10},{10,1... | collective-permute-start | bytes 98312 | tf_op jit(solution)/shard_map/ppermute | solution.py:55
  92.9 8.3 %copy-start.5 = (f32[128,128]{1,0:T(8,128)S(1)}, f32[128,128]{1,0:T(8,128)}, u32[]{:S(2)}) copy-start(f32[128,128]{1,0:T(8,128)} %param.24) | copy-start | bytes 196612
  92.9 8.3 %copy-start.6 = (f32[128,128]{1,0:T(8,128)S(1)}, f32[128,128]{1,0:T(8,128)}, u32[]{:S(2)}) copy-start(f32[128,128]{1,0:T(8,128)} %param.25) | copy-start | bytes 196612
  92.9 8.3 %copy-start.7 = (f32[128,128]{1,0:T(8,128)S(1)}, f32[128,128]{1,0:T(8,128)}, u32[]{:S(2)}) copy-start(f32[128,128]{1,0:T(8,128)} %param.23) | copy-start | bytes 196612
  92.9 8.3 %copy-start.14 = (s32[128]{0:T(128)S(1)}, s32[128]{0:T(128)}, u32[]{:S(2)}) copy-start(s32[128]{0:T(128)} %param.29) | copy-start | bytes 1540
  106.8 31.3 %collective-permute-start.4 = (f32[3,3]{1,0:T(4,128)S(1)}, f32[3,3]{1,0:T(4,128)S(1)}, u32[]{:S(2)}, u32[]{:S(2)}) collective-permute-start(f32[3,3]{1,0:T(4,128)S(1)} %slice.142), channel_id=1, source_target_pairs={{0,1},{1,2},{2,3},{3,4},{4,5},{5,6},{6,7},{7,8},{8,9},{9,10},{10,1... | collective-permute-start | bytes 116 | tf_op jit(solution)/shard_map/ppermute | solution.py:12
  122.3 143.1 %copy-start.11 = (f32[5,128]{1,0:T(8,128)S(1)}, f32[5,128]{1,0:T(8,128)}, u32[]{:S(2)}) copy-start(f32[5,128]{1,0:T(8,128)} %param.30) | copy-start | bytes 7684
  122.3 143.7 %copy-start.4 = (f32[2,4096]{1,0:T(2,128)S(1)}, f32[2,4096]{1,0:T(2,128)}, u32[]{:S(2)}) copy-start(f32[2,4096]{1,0:T(2,128)} %param.32) | copy-start | bytes 98308
  122.3 145.1 %copy-start.12 = (f32[3,128]{1,0:T(4,128)S(1)}, f32[3,128]{1,0:T(4,128)}, u32[]{:S(2)}) copy-start(f32[3,128]{1,0:T(4,128)} %param.31) | copy-start | bytes 4612
  266.0 49.2 %copy-start.10 = (f32[5,128]{1,0:T(8,128)}, f32[5,128]{1,0:T(8,128)S(1)}, u32[]{:S(2)}) copy-start(f32[5,128]{1,0:T(8,128)S(1)} %get-tuple-element.51) | copy-start | bytes 7684
  266.7 48.5 %copy-start.3 = (f32[2,4096]{1,0:T(2,128)}, f32[2,4096]{1,0:T(2,128)S(1)}, u32[]{:S(2)}) copy-start(f32[2,4096]{1,0:T(2,128)S(1)} %get-tuple-element.47) | copy-start | bytes 98308
  268.2 47.1 %copy-start.13 = (f32[3,128]{1,0:T(4,128)}, f32[3,128]{1,0:T(4,128)S(1)}, u32[]{:S(2)}) copy-start(f32[3,128]{1,0:T(4,128)S(1)} %get-tuple-element.49) | copy-start | bytes 4612
Sparse Core Ops, SparseCore 0:
  138.2 123.6 all-reduce.7
